TPU v7x, 256 devices: a whole 4x4x8 slice. The times are simulated.
256 devices in a mesh: ctx: 32 (over x, z), head: 8 (over y, core).
Axes of the slice: x: 4, y: 4, z: 8, core: 2. Of those that a mesh axis runs over, the one named last changes fastest.
Arguments:
- query_in: bfloat16 [16384, 2048], P('ctx', 'head'), may hold values from -6 to 6
- key_in: bfloat16 [16384, 2048], P('ctx', 'head'), may hold values from -6 to 6
- value_in: bfloat16 [16384, 4096], P('ctx', 'head'), may hold values from -6 to 6
- query_taps: float32 [4, 2048], P(None, 'head'), may hold values from -3 to 3
- key_taps: float32 [4, 2048], P(None, 'head'), may hold values from -3 to 3
- value_taps: float32 [4, 4096], P(None, 'head'), may hold values from -3 to 3
- log_decay: float32 [32, 16384], P('head', 'ctx'), may hold values from -2 to 0
- beta_logit: float32 [32, 16384], P('head', 'ctx'), may hold values from -9 to 2
- gate_in: bfloat16 [16384, 4096], P('ctx', 'head'), may hold values from -6 to 6
- norm_gain: float32 [128], replicated, may hold values from 0.1 to 1.9
Outputs:
- core_out: bfloat16 [16384, 4096], P(('ctx', 'head'))
All inputs are finite; a program needn't handle non-finite values.
Results may differ from a plain program's by a relative error of at most 0.005.
Values may be sent and summed in bfloat16 or wider, within the bound.
No kernel may reach another device: no remote copies, remote signals or barrier semaphores. Data moves between devices by JAX's collectives and lax.ppermute only.
A program may use at most 64 MiB of HBM per device.

v0:
```python
import jax
import jax.numpy as jnp
from jax import lax
from jax.sharding import PartitionSpec as P

GROUP = 64
highest = lax.Precision.HIGHEST
norm_eps = 1e-06


def shifted(value, axis, steps):
    count = lax.axis_size(axis)
    first, last = (max(0, -steps), min(count, count - steps))
    return lax.ppermute(value, axis, [(source, source + steps) for source in range(first, last)])


def causal_conv(joined, taps, length):
    summed = jnp.zeros((length, joined.shape[1]), jnp.float32)
    for offset in range(taps.shape[0]):
        summed = summed + taps[offset] * joined[offset : offset + length].astype(jnp.float32)
    return jax.nn.silu(summed)


def unit_rows(matrix):
    return matrix * lax.rsqrt(jnp.sum(matrix * matrix, axis=-1, keepdims=True) + norm_eps)


def group_terms(query, keys, values, beta, logdecay):
    length = logdecay.shape[-1]
    cumul = jnp.cumsum(logdecay, axis=-1)
    row_ids = lax.broadcasted_iota(jnp.int32, (length, length), 0)
    col_ids = lax.broadcasted_iota(jnp.int32, (length, length), 1)
    inside = col_ids <= row_ids
    differ = cumul[..., :, None] - cumul[..., None, :]
    decay_mask = jnp.where(inside, jnp.exp(jnp.where(inside, differ, 0.0)), 0.0)
    keygram = jnp.einsum("...ik,...jk->...ij", keys, keys, precision=highest)
    strict = jnp.where(col_ids < row_ids, beta[..., :, None] * keygram * decay_mask, 0.0)
    identity_mats = jnp.broadcast_to(jnp.eye(length, dtype=jnp.float32), strict.shape)
    inverse = lax.linalg.triangular_solve(
        identity_mats + strict, identity_mats, left_side=True, lower=True, unit_diagonal=True
    )
    upd_values = jnp.einsum(
        "...ij,...jd->...id", inverse, beta[..., None] * values, precision=highest
    )
    upd_keys = jnp.einsum(
        "...ij,...jd->...id", inverse, (beta * jnp.exp(cumul))[..., None] * keys, precision=highest
    )
    scores = jnp.einsum("...ik,...jk->...ij", query, keys, precision=highest) * decay_mask
    last_log = cumul[..., -1:]
    query_decay = query * jnp.exp(cumul)[..., None]
    key_decay = keys * jnp.exp(last_log - cumul)[..., None]
    return (upd_values, upd_keys, scores, query_decay, key_decay, last_log[..., 0])


def group_step(state, terms):
    upd_values, upd_keys, scores, query_decay, key_decay, last_log = terms
    new_values = upd_values - jnp.einsum("...ik,...kd->...id", upd_keys, state, precision=highest)
    output = jnp.einsum("...ik,...kd->...id", query_decay, state, precision=highest)
    output = output + jnp.einsum("...ij,...jd->...id", scores, new_values, precision=highest)
    state = jnp.exp(last_log)[..., None, None] * state + jnp.einsum(
        "...ik,...id->...kd", key_decay, new_values, precision=highest
    )
    return (state, output)


def matmul_pair(left_mats, right_mats):
    return jnp.einsum("...ij,...jk->...ik", left_mats, right_mats, precision=highest)


def body(
    query_in,
    key_in,
    value_in,
    query_taps,
    key_taps,
    value_taps,
    log_decay,
    beta_logit,
    gate_in,
    norm_gain,
):
    head_size = norm_gain.shape[0]
    length = query_in.shape[0]
    value_heads = log_decay.shape[0]
    key_heads = query_in.shape[1] // head_size
    share_ratio = value_heads // key_heads
    rim_width = query_taps.shape[0] - 1
    groups_dev = length // GROUP
    tail_rows = shifted(
        (
            query_in[length - rim_width :],
            key_in[length - rim_width :],
            value_in[length - rim_width :],
        ),
        "ctx",
        1,
    )
    query_conv = causal_conv(jnp.concatenate([tail_rows[0], query_in], axis=0), query_taps, length)
    key_conv = causal_conv(jnp.concatenate([tail_rows[1], key_in], axis=0), key_taps, length)
    value_conv = causal_conv(jnp.concatenate([tail_rows[2], value_in], axis=0), value_taps, length)
    queries = (
        unit_rows(query_conv.reshape(length, key_heads, head_size)) * head_size ** (-0.5)
    ).astype(jnp.bfloat16)
    keys = unit_rows(key_conv.reshape(length, key_heads, head_size)).astype(jnp.bfloat16)
    values = value_conv.reshape(length, value_heads, head_size).astype(jnp.bfloat16)

    def blocked(array):
        return (
            array.astype(jnp.float32)
            .reshape(groups_dev, GROUP, array.shape[1], head_size)
            .transpose(0, 2, 1, 3)
        )

    def blocked_rates(array):
        return array.reshape(value_heads, groups_dev, GROUP).transpose(1, 0, 2)

    query_blocks = blocked(jnp.repeat(queries, share_ratio, axis=1))
    key_blocks = blocked(jnp.repeat(keys, share_ratio, axis=1))
    value_blocks = blocked(values)
    beta_blocks = blocked_rates(jax.nn.sigmoid(beta_logit))
    decay_blocks = blocked_rates(log_decay)
    terms = group_terms(query_blocks, key_blocks, value_blocks, beta_blocks, decay_blocks)
    upd_values, upd_keys, scores, query_decay, key_decay, last_log = terms
    identity_state = jnp.broadcast_to(
        jnp.eye(head_size, dtype=jnp.float32), (value_heads, head_size, head_size)
    )
    group_maps = jnp.exp(last_log)[..., None, None] * identity_state - jnp.einsum(
        "...ik,...ij->...kj", key_decay, upd_keys, precision=highest
    )
    query_effect = query_decay - matmul_pair(scores, upd_keys)

    def local_step(carry, packed):
        state, product = carry
        group, group_map = packed
        state, output = group_step(state, group)
        return ((state, matmul_pair(group_map, product)), output)

    zero_state = jnp.zeros((value_heads, head_size, head_size), jnp.float32)
    (local_state, shard_map_mat), local_out = lax.scan(
        local_step, (zero_state, identity_state), (terms, group_maps)
    )

    def chain_turn(turn, incoming_state):
        return shifted(matmul_pair(shard_map_mat, incoming_state) + local_state, "ctx", 1)

    incoming = lax.fori_loop(0, lax.axis_size("ctx") - 1, chain_turn, zero_state)

    def carried_step(state, packed):
        effect_group, group_map = packed
        return (matmul_pair(group_map, state), matmul_pair(effect_group, state))

    _, carried_out = lax.scan(carried_step, incoming, (query_effect, group_maps))
    output = (local_out + carried_out).transpose(0, 2, 1, 3).reshape(length, value_heads, head_size)
    gates = gate_in.reshape(length, value_heads, head_size).astype(jnp.float32)
    normed = (
        output
        * lax.rsqrt(jnp.mean(output * output, axis=-1, keepdims=True) + norm_eps)
        * norm_gain
        * jax.nn.silu(gates)
    )
    normed = normed.astype(jnp.bfloat16).reshape(length, value_heads * head_size)
    return lax.all_to_all(normed, "head", split_axis=0, concat_axis=1, tiled=True)


def solution(mesh):
    in_specs = (
        P("ctx", "head"),
        P("ctx", "head"),
        P("ctx", "head"),
        P(None, "head"),
        P(None, "head"),
        P(None, "head"),
        P("head", "ctx"),
        P("head", "ctx"),
        P("ctx", "head"),
        P(),
    )
    out_specs = P(("ctx", "head"), None)
    return jax.shard_map(body, mesh=mesh, in_specs=in_specs, out_specs=out_specs, check_vma=False)
```

profile of v0, /device:TPU:2, one launch (start us, length us, event | category | flops | bytes accessed | tf_op | source)
XLA Modules:
  0.0 657.1 jit_solution(1488363138327916721)
XLA Ops:
  23.5 157.3 %custom-call.3 = f32[8,4,1,64,64]{3,4,2,1,0:T(8,128)S(1)} custom-call(f32[8,4,1,64,64]{4,3,2,1,0:T(8,128)S(1)} %fusion.42), custom_call_target="InvertDiagBlocksLowerTriangular" | custom-call | tf_op jit(solution)/shard_map/triangular_solve | solution.py:39
  204.8 53.3 %while.39 = (s32[]{:T(128)}, f32[4,128,128]{2,1,0:T(8,128)S(1)}, f32[4,128,128]{2,1,0:T(8,128)S(1)}, f32[8,4,64,128]{3,2,1,0:T(8,128)S(1)}, f32[8,4]{1,0:T(8,128...) while((s32[]{:T(128)}, f32[4,128,128]{2,1,0:T(8,128)S(1)}, ...), condition=%wide.region_4.5_spmd.clone, body=%wide.region_3.4_spmd.clone.sunk | while | flops 277217280 | bytes 3804367 | solution.py:139
  258.1 357.7 %while.37 = (s32[]{:T(128)}, f32[4,128,128]{2,1,0:T(8,128)S(1)}, f32[4,128,128]{2,1,0:T(8,128)S(1)}, f32[4,128,128]{2,1,0:T(8,128)S(1)}, s32[]{:T(128)}) while((s32[]{:T(128)}, f32[4,128,128]{2,1,0:T(8,128)S(1)}, f32[4,128,128]{2,1,0:T(8,128)S(1)}, f32[4,128,128]{2,1,0:T(8,128)S(1)}, s32[]{:T(128)}) %tuple.71), condition=%wide.region_6.7_spmd, body=%wide.region_5.6_spmd.sunk | while | flops 100728832 | bytes 2097253 | solution.py:146
  283.1 8.4 %collective-permute-done = f32[4,128,128]{2,1,0:T(8,128)S(1)} collective-permute-done((f32[4,128,128]{2,1,0:T(8,128)S(1)}, f32[4,128,128]{2,1,0:T(8,128)S(1)}, u32[]{:S(2)}, u32[]{:S(2)}) %collective-permute-start) | collective-permute-done | bytes 262176 | tf_op jit(solution)/shard_map/while/body/eval_jaxpr/ppermute | solution.py:14
  293.9 8.4 %collective-permute-done = f32[4,128,128]{2,1,0:T(8,128)S(1)} collective-permute-done((f32[4,128,128]{2,1,0:T(8,128)S(1)}, f32[4,128,128]{2,1,0:T(8,128)S(1)}, u32[]{:S(2)}, u32[]{:S(2)}) %collective-permute-start) | collective-permute-done | bytes 262176 | tf_op jit(solution)/shard_map/while/body/eval_jaxpr/ppermute | solution.py:14
  304.7 8.4 %collective-permute-done = f32[4,128,128]{2,1,0:T(8,128)S(1)} collective-permute-done((f32[4,128,128]{2,1,0:T(8,128)S(1)}, f32[4,128,128]{2,1,0:T(8,128)S(1)}, u32[]{:S(2)}, u32[]{:S(2)}) %collective-permute-start) | collective-permute-done | bytes 262176 | tf_op jit(solution)/shard_map/while/body/eval_jaxpr/ppermute | solution.py:14
  315.5 9.1 %collective-permute-done = f32[4,128,128]{2,1,0:T(8,128)S(1)} collective-permute-done((f32[4,128,128]{2,1,0:T(8,128)S(1)}, f32[4,128,128]{2,1,0:T(8,128)S(1)}, u32[]{:S(2)}, u32[]{:S(2)}) %collective-permute-start) | collective-permute-done | bytes 262176 | tf_op jit(solution)/shard_map/while/body/eval_jaxpr/ppermute | solution.py:14
  326.8 10.2 %collective-permute-done = f32[4,128,128]{2,1,0:T(8,128)S(1)} collective-permute-done((f32[4,128,128]{2,1,0:T(8,128)S(1)}, f32[4,128,128]{2,1,0:T(8,128)S(1)}, u32[]{:S(2)}, u32[]{:S(2)}) %collective-permute-start) | collective-permute-done | bytes 262176 | tf_op jit(solution)/shard_map/while/body/eval_jaxpr/ppermute | solution.py:14
  339.4 11.2 %collective-permute-done = f32[4,128,128]{2,1,0:T(8,128)S(1)} collective-permute-done((f32[4,128,128]{2,1,0:T(8,128)S(1)}, f32[4,128,128]{2,1,0:T(8,128)S(1)}, u32[]{:S(2)}, u32[]{:S(2)}) %collective-permute-start) | collective-permute-done | bytes 262176 | tf_op jit(solution)/shard_map/while/body/eval_jaxpr/ppermute | solution.py:14
  352.9 10.3 %collective-permute-done = f32[4,128,128]{2,1,0:T(8,128)S(1)} collective-permute-done((f32[4,128,128]{2,1,0:T(8,128)S(1)}, f32[4,128,128]{2,1,0:T(8,128)S(1)}, u32[]{:S(2)}, u32[]{:S(2)}) %collective-permute-start) | collective-permute-done | bytes 262176 | tf_op jit(solution)/shard_map/while/body/eval_jaxpr/ppermute | solution.py:14
  365.5 9.4 %collective-permute-done = f32[4,128,128]{2,1,0:T(8,128)S(1)} collective-permute-done((f32[4,128,128]{2,1,0:T(8,128)S(1)}, f32[4,128,128]{2,1,0:T(8,128)S(1)}, u32[]{:S(2)}, u32[]{:S(2)}) %collective-permute-start) | collective-permute-done | bytes 262176 | tf_op jit(solution)/shard_map/while/body/eval_jaxpr/ppermute | solution.py:14
  377.3 8.6 %collective-permute-done = f32[4,128,128]{2,1,0:T(8,128)S(1)} collective-permute-done((f32[4,128,128]{2,1,0:T(8,128)S(1)}, f32[4,128,128]{2,1,0:T(8,128)S(1)}, u32[]{:S(2)}, u32[]{:S(2)}) %collective-permute-start) | collective-permute-done | bytes 262176 | tf_op jit(solution)/shard_map/while/body/eval_jaxpr/ppermute | solution.py:14
  388.2 8.4 %collective-permute-done = f32[4,128,128]{2,1,0:T(8,128)S(1)} collective-permute-done((f32[4,128,128]{2,1,0:T(8,128)S(1)}, f32[4,128,128]{2,1,0:T(8,128)S(1)}, u32[]{:S(2)}, u32[]{:S(2)}) %collective-permute-start) | collective-permute-done | bytes 262176 | tf_op jit(solution)/shard_map/while/body/eval_jaxpr/ppermute | solution.py:14
  399.0 8.4 %collective-permute-done = f32[4,128,128]{2,1,0:T(8,128)S(1)} collective-permute-done((f32[4,128,128]{2,1,0:T(8,128)S(1)}, f32[4,128,128]{2,1,0:T(8,128)S(1)}, u32[]{:S(2)}, u32[]{:S(2)}) %collective-permute-start) | collective-permute-done | bytes 262176 | tf_op jit(solution)/shard_map/while/body/eval_jaxpr/ppermute | solution.py:14
  409.8 8.4 %collective-permute-done = f32[4,128,128]{2,1,0:T(8,128)S(1)} collective-permute-done((f32[4,128,128]{2,1,0:T(8,128)S(1)}, f32[4,128,128]{2,1,0:T(8,128)S(1)}, u32[]{:S(2)}, u32[]{:S(2)}) %collective-permute-start) | collective-permute-done | bytes 262176 | tf_op jit(solution)/shard_map/while/body/eval_jaxpr/ppermute | solution.py:14
  420.6 8.6 %collective-permute-done = f32[4,128,128]{2,1,0:T(8,128)S(1)} collective-permute-done((f32[4,128,128]{2,1,0:T(8,128)S(1)}, f32[4,128,128]{2,1,0:T(8,128)S(1)}, u32[]{:S(2)}, u32[]{:S(2)}) %collective-permute-start) | collective-permute-done | bytes 262176 | tf_op jit(solution)/shard_map/while/body/eval_jaxpr/ppermute | solution.py:14
  431.5 9.7 %collective-permute-done = f32[4,128,128]{2,1,0:T(8,128)S(1)} collective-permute-done((f32[4,128,128]{2,1,0:T(8,128)S(1)}, f32[4,128,128]{2,1,0:T(8,128)S(1)}, u32[]{:S(2)}, u32[]{:S(2)}) %collective-permute-start) | collective-permute-done | bytes 262176 | tf_op jit(solution)/shard_map/while/body/eval_jaxpr/ppermute | solution.py:14
  443.5 10.9 %collective-permute-done = f32[4,128,128]{2,1,0:T(8,128)S(1)} collective-permute-done((f32[4,128,128]{2,1,0:T(8,128)S(1)}, f32[4,128,128]{2,1,0:T(8,128)S(1)}, u32[]{:S(2)}, u32[]{:S(2)}) %collective-permute-start) | collective-permute-done | bytes 262176 | tf_op jit(solution)/shard_map/while/body/eval_jaxpr/ppermute | solution.py:14
  456.8 10.5 %collective-permute-done = f32[4,128,128]{2,1,0:T(8,128)S(1)} collective-permute-done((f32[4,128,128]{2,1,0:T(8,128)S(1)}, f32[4,128,128]{2,1,0:T(8,128)S(1)}, u32[]{:S(2)}, u32[]{:S(2)}) %collective-permute-start) | collective-permute-done | bytes 262176 | tf_op jit(solution)/shard_map/while/body/eval_jaxpr/ppermute | solution.py:14
  469.6 9.6 %collective-permute-done = f32[4,128,128]{2,1,0:T(8,128)S(1)} collective-permute-done((f32[4,128,128]{2,1,0:T(8,128)S(1)}, f32[4,128,128]{2,1,0:T(8,128)S(1)}, u32[]{:S(2)}, u32[]{:S(2)}) %collective-permute-start) | collective-permute-done | bytes 262176 | tf_op jit(solution)/shard_map/while/body/eval_jaxpr/ppermute | solution.py:14
  481.5 8.8 %collective-permute-done = f32[4,128,128]{2,1,0:T(8,128)S(1)} collective-permute-done((f32[4,128,128]{2,1,0:T(8,128)S(1)}, f32[4,128,128]{2,1,0:T(8,128)S(1)}, u32[]{:S(2)}, u32[]{:S(2)}) %collective-permute-start) | collective-permute-done | bytes 262176 | tf_op jit(solution)/shard_map/while/body/eval_jaxpr/ppermute | solution.py:14
  492.6 8.4 %collective-permute-done = f32[4,128,128]{2,1,0:T(8,128)S(1)} collective-permute-done((f32[4,128,128]{2,1,0:T(8,128)S(1)}, f32[4,128,128]{2,1,0:T(8,128)S(1)}, u32[]{:S(2)}, u32[]{:S(2)}) %collective-permute-start) | collective-permute-done | bytes 262176 | tf_op jit(solution)/shard_map/while/body/eval_jaxpr/ppermute | solution.py:14
  514.2 8.4 %collective-permute-done = f32[4,128,128]{2,1,0:T(8,128)S(1)} collective-permute-done((f32[4,128,128]{2,1,0:T(8,128)S(1)}, f32[4,128,128]{2,1,0:T(8,128)S(1)}, u32[]{:S(2)}, u32[]{:S(2)}) %collective-permute-start) | collective-permute-done | bytes 262176 | tf_op jit(solution)/shard_map/while/body/eval_jaxpr/ppermute | solution.py:14
  535.8 9.6 %collective-permute-done = f32[4,128,128]{2,1,0:T(8,128)S(1)} collective-permute-done((f32[4,128,128]{2,1,0:T(8,128)S(1)}, f32[4,128,128]{2,1,0:T(8,128)S(1)}, u32[]{:S(2)}, u32[]{:S(2)}) %collective-permute-start) | collective-permute-done | bytes 262176 | tf_op jit(solution)/shard_map/while/body/eval_jaxpr/ppermute | solution.py:14
  547.7 10.7 %collective-permute-done = f32[4,128,128]{2,1,0:T(8,128)S(1)} collective-permute-done((f32[4,128,128]{2,1,0:T(8,128)S(1)}, f32[4,128,128]{2,1,0:T(8,128)S(1)}, u32[]{:S(2)}, u32[]{:S(2)}) %collective-permute-start) | collective-permute-done | bytes 262176 | tf_op jit(solution)/shard_map/while/body/eval_jaxpr/ppermute | solution.py:14
  560.7 10.6 %collective-permute-done = f32[4,128,128]{2,1,0:T(8,128)S(1)} collective-permute-done((f32[4,128,128]{2,1,0:T(8,128)S(1)}, f32[4,128,128]{2,1,0:T(8,128)S(1)}, u32[]{:S(2)}, u32[]{:S(2)}) %collective-permute-start) | collective-permute-done | bytes 262176 | tf_op jit(solution)/shard_map/while/body/eval_jaxpr/ppermute | solution.py:14
  573.7 9.8 %collective-permute-done = f32[4,128,128]{2,1,0:T(8,128)S(1)} collective-permute-done((f32[4,128,128]{2,1,0:T(8,128)S(1)}, f32[4,128,128]{2,1,0:T(8,128)S(1)}, u32[]{:S(2)}, u32[]{:S(2)}) %collective-permute-start) | collective-permute-done | bytes 262176 | tf_op jit(solution)/shard_map/while/body/eval_jaxpr/ppermute | solution.py:14
  585.8 8.4 %collective-permute-done = f32[4,128,128]{2,1,0:T(8,128)S(1)} collective-permute-done((f32[4,128,128]{2,1,0:T(8,128)S(1)}, f32[4,128,128]{2,1,0:T(8,128)S(1)}, u32[]{:S(2)}, u32[]{:S(2)}) %collective-permute-start) | collective-permute-done | bytes 262176 | tf_op jit(solution)/shard_map/while/body/eval_jaxpr/ppermute | solution.py:14
  596.6 8.4 %collective-permute-done = f32[4,128,128]{2,1,0:T(8,128)S(1)} collective-permute-done((f32[4,128,128]{2,1,0:T(8,128)S(1)}, f32[4,128,128]{2,1,0:T(8,128)S(1)}, u32[]{:S(2)}, u32[]{:S(2)}) %collective-permute-start) | collective-permute-done | bytes 262176 | tf_op jit(solution)/shard_map/while/body/eval_jaxpr/ppermute | solution.py:14
  607.4 8.4 %collective-permute-done = f32[4,128,128]{2,1,0:T(8,128)S(1)} collective-permute-done((f32[4,128,128]{2,1,0:T(8,128)S(1)}, f32[4,128,128]{2,1,0:T(8,128)S(1)}, u32[]{:S(2)}, u32[]{:S(2)}) %collective-permute-start) | collective-permute-done | bytes 262176 | tf_op jit(solution)/shard_map/while/body/eval_jaxpr/ppermute | solution.py:14
  615.9 21.4 %while.38 = (s32[]{:T(128)}, f32[4,128,128]{2,1,0:T(8,128)S(1)}, f32[8,4,64,128]{3,2,1,0:T(8,128)S(1)}, f32[8,4,128,128]{3,2,1,0:T(8,128)}, f32[8,4,64,128]{3,2,1,0:T(8,128)}, /*index=5*/s32[]{:T(128)}) while((s32[]{:T(128)}, f32[4,128,128]{2,1,0:T(8,128)S(1)}, f32[8,4,64,128]{3,2,1,0:T(8,128)S(1)}, f32[8,4,128,128]{3,2,1,0:T(8,128)}, ...), condition=%wide.region_8.9_spmd, body=%wide.region_7.8_spmd.sunk | while | flops 150994944 | bytes 1836113 | solution.py:152
  641.6 14.6 %all_to_all.19 = bf16[8,64,512]{2,1,0:T(8,128)(2,1)S(1)} all-to-all(bf16[8,64,512]{2,1,0:T(8,128)(2,1)S(1)} %bitcast.148), channel_id=1, replica_groups=mesh['ctx'=32,'head'=8] {'head'}, dimensions={0} | all-to-all | bytes 1048576 | tf_op jit(solution)/shard_map/all_to_all | solution.py:162
  (224 shorter events, 232.8 us)
Async XLA Ops:
  0.7 18.5 %collective-permute-start.1 = (bf16[3,256]{1,0:T(4,128)(2,1)S(1)}, bf16[3,256]{1,0:T(4,128)(2,1)S(1)}, u32[]{:S(2)}, u32[]{:S(2)}) collective-permute-start(bf16[3,256]{1,0:T(4,128)(2,1)S(1)} %slice.81), channel_id=1, source_target_pairs={{0,8},{8,16},{16,24},{24,32},{32,40},{40,48},{48,56},{56,64},{64,7... | collective-permute-start | bytes 4616 | tf_op jit(solution)/shard_map/ppermute | solution.py:14
  5.2 191.8 %collective-permute-start.2 = (bf16[3,512]{1,0:T(4,128)(2,1)S(1)}, bf16[3,512]{1,0:T(4,128)(2,1)S(1)}, u32[]{:S(2)}, u32[]{:S(2)}) collective-permute-start(bf16[3,512]{1,0:T(4,128)(2,1)S(1)} %slice.89), channel_id=1, source_target_pairs={{0,8},{8,16},{16,24},{24,32},{32,40},{40,48},{48,56},{56,64},{64,7... | collective-permute-start | bytes 9224 | tf_op jit(solution)/shard_map/ppermute | solution.py:14
  9.8 172.9 %collective-permute-start.3 = (bf16[3,256]{1,0:T(4,128)(2,1)S(1)}, bf16[3,256]{1,0:T(4,128)(2,1)S(1)}, u32[]{:S(2)}, u32[]{:S(2)}) collective-permute-start(bf16[3,256]{1,0:T(4,128)(2,1)S(1)} %slice.97), channel_id=1, source_target_pairs={{0,8},{8,16},{16,24},{24,32},{32,40},{40,48},{48,56},{56,64},{64,7... | collective-permute-start | bytes 4616 | tf_op jit(solution)/shard_map/ppermute | solution.py:14
  258.8 11.2 %collective-permute-start = (f32[4,128,128]{2,1,0:T(8,128)S(1)}, f32[4,128,128]{2,1,0:T(8,128)S(1)}, u32[]{:S(2)}, u32[]{:S(2)}) collective-permute-start(f32[4,128,128]{2,1,0:T(8,128)S(1)} %convolution_add_fusion.5), channel_id=1, source_target_pairs={{0,8},{8,16},{16,24},{24,32},{32,40},{40,48},{48,56},{56,64},{64,7... | collective-permute-start | bytes 786440 | tf_op jit(solution)/shard_map/while/body/eval_jaxpr/ppermute | solution.py:14
  270.4 10.4 %collective-permute-start = (f32[4,128,128]{2,1,0:T(8,128)S(1)}, f32[4,128,128]{2,1,0:T(8,128)S(1)}, u32[]{:S(2)}, u32[]{:S(2)}) collective-permute-start(f32[4,128,128]{2,1,0:T(8,128)S(1)} %convolution_add_fusion.5), channel_id=1, source_target_pairs={{0,8},{8,16},{16,24},{24,32},{32,40},{40,48},{48,56},{56,64},{64,7... | collective-permute-start | bytes 786440 | tf_op jit(solution)/shard_map/while/body/eval_jaxpr/ppermute | solution.py:14
  281.2 10.4 %collective-permute-start = (f32[4,128,128]{2,1,0:T(8,128)S(1)}, f32[4,128,128]{2,1,0:T(8,128)S(1)}, u32[]{:S(2)}, u32[]{:S(2)}) collective-permute-start(f32[4,128,128]{2,1,0:T(8,128)S(1)} %convolution_add_fusion.5), channel_id=1, source_target_pairs={{0,8},{8,16},{16,24},{24,32},{32,40},{40,48},{48,56},{56,64},{64,7... | collective-permute-start | bytes 786440 | tf_op jit(solution)/shard_map/while/body/eval_jaxpr/ppermute | solution.py:14
  292.0 10.4 %collective-permute-start = (f32[4,128,128]{2,1,0:T(8,128)S(1)}, f32[4,128,128]{2,1,0:T(8,128)S(1)}, u32[]{:S(2)}, u32[]{:S(2)}) collective-permute-start(f32[4,128,128]{2,1,0:T(8,128)S(1)} %convolution_add_fusion.5), channel_id=1, source_target_pairs={{0,8},{8,16},{16,24},{24,32},{32,40},{40,48},{48,56},{56,64},{64,7... | collective-permute-start | bytes 786440 | tf_op jit(solution)/shard_map/while/body/eval_jaxpr/ppermute | solution.py:14
  302.7 10.4 %collective-permute-start = (f32[4,128,128]{2,1,0:T(8,128)S(1)}, f32[4,128,128]{2,1,0:T(8,128)S(1)}, u32[]{:S(2)}, u32[]{:S(2)}) collective-permute-start(f32[4,128,128]{2,1,0:T(8,128)S(1)} %convolution_add_fusion.5), channel_id=1, source_target_pairs={{0,8},{8,16},{16,24},{24,32},{32,40},{40,48},{48,56},{56,64},{64,7... | collective-permute-start | bytes 786440 | tf_op jit(solution)/shard_map/while/body/eval_jaxpr/ppermute | solution.py:14
  313.5 11.0 %collective-permute-start = (f32[4,128,128]{2,1,0:T(8,128)S(1)}, f32[4,128,128]{2,1,0:T(8,128)S(1)}, u32[]{:S(2)}, u32[]{:S(2)}) collective-permute-start(f32[4,128,128]{2,1,0:T(8,128)S(1)} %convolution_add_fusion.5), channel_id=1, source_target_pairs={{0,8},{8,16},{16,24},{24,32},{32,40},{40,48},{48,56},{56,64},{64,7... | collective-permute-start | bytes 786440 | tf_op jit(solution)/shard_map/while/body/eval_jaxpr/ppermute | solution.py:14
  324.9 12.1 %collective-permute-start = (f32[4,128,128]{2,1,0:T(8,128)S(1)}, f32[4,128,128]{2,1,0:T(8,128)S(1)}, u32[]{:S(2)}, u32[]{:S(2)}) collective-permute-start(f32[4,128,128]{2,1,0:T(8,128)S(1)} %convolution_add_fusion.5), channel_id=1, source_target_pairs={{0,8},{8,16},{16,24},{24,32},{32,40},{40,48},{48,56},{56,64},{64,7... | collective-permute-start | bytes 786440 | tf_op jit(solution)/shard_map/while/body/eval_jaxpr/ppermute | solution.py:14
  337.4 13.1 %collective-permute-start = (f32[4,128,128]{2,1,0:T(8,128)S(1)}, f32[4,128,128]{2,1,0:T(8,128)S(1)}, u32[]{:S(2)}, u32[]{:S(2)}) collective-permute-start(f32[4,128,128]{2,1,0:T(8,128)S(1)} %convolution_add_fusion.5), channel_id=1, source_target_pairs={{0,8},{8,16},{16,24},{24,32},{32,40},{40,48},{48,56},{56,64},{64,7... | collective-permute-start | bytes 786440 | tf_op jit(solution)/shard_map/while/body/eval_jaxpr/ppermute | solution.py:14
  350.9 12.2 %collective-permute-start = (f32[4,128,128]{2,1,0:T(8,128)S(1)}, f32[4,128,128]{2,1,0:T(8,128)S(1)}, u32[]{:S(2)}, u32[]{:S(2)}) collective-permute-start(f32[4,128,128]{2,1,0:T(8,128)S(1)} %convolution_add_fusion.5), channel_id=1, source_target_pairs={{0,8},{8,16},{16,24},{24,32},{32,40},{40,48},{48,56},{56,64},{64,7... | collective-permute-start | bytes 786440 | tf_op jit(solution)/shard_map/while/body/eval_jaxpr/ppermute | solution.py:14
  363.6 11.4 %collective-permute-start = (f32[4,128,128]{2,1,0:T(8,128)S(1)}, f32[4,128,128]{2,1,0:T(8,128)S(1)}, u32[]{:S(2)}, u32[]{:S(2)}) collective-permute-start(f32[4,128,128]{2,1,0:T(8,128)S(1)} %convolution_add_fusion.5), channel_id=1, source_target_pairs={{0,8},{8,16},{16,24},{24,32},{32,40},{40,48},{48,56},{56,64},{64,7... | collective-permute-start | bytes 786440 | tf_op jit(solution)/shard_map/while/body/eval_jaxpr/ppermute | solution.py:14
  375.4 10.5 %collective-permute-start = (f32[4,128,128]{2,1,0:T(8,128)S(1)}, f32[4,128,128]{2,1,0:T(8,128)S(1)}, u32[]{:S(2)}, u32[]{:S(2)}) collective-permute-start(f32[4,128,128]{2,1,0:T(8,128)S(1)} %convolution_add_fusion.5), channel_id=1, source_target_pairs={{0,8},{8,16},{16,24},{24,32},{32,40},{40,48},{48,56},{56,64},{64,7... | collective-permute-start | bytes 786440 | tf_op jit(solution)/shard_map/while/body/eval_jaxpr/ppermute | solution.py:14
  386.3 10.4 %collective-permute-start = (f32[4,128,128]{2,1,0:T(8,128)S(1)}, f32[4,128,128]{2,1,0:T(8,128)S(1)}, u32[]{:S(2)}, u32[]{:S(2)}) collective-permute-start(f32[4,128,128]{2,1,0:T(8,128)S(1)} %convolution_add_fusion.5), channel_id=1, source_target_pairs={{0,8},{8,16},{16,24},{24,32},{32,40},{40,48},{48,56},{56,64},{64,7... | collective-permute-start | bytes 786440 | tf_op jit(solution)/shard_map/while/body/eval_jaxpr/ppermute | solution.py:14
  397.1 10.4 %collective-permute-start = (f32[4,128,128]{2,1,0:T(8,128)S(1)}, f32[4,128,128]{2,1,0:T(8,128)S(1)}, u32[]{:S(2)}, u32[]{:S(2)}) collective-permute-start(f32[4,128,128]{2,1,0:T(8,128)S(1)} %convolution_add_fusion.5), channel_id=1, source_target_pairs={{0,8},{8,16},{16,24},{24,32},{32,40},{40,48},{48,56},{56,64},{64,7... | collective-permute-start | bytes 786440 | tf_op jit(solution)/shard_map/while/body/eval_jaxpr/ppermute | solution.py:14
  407.8 10.4 %collective-permute-start = (f32[4,128,128]{2,1,0:T(8,128)S(1)}, f32[4,128,128]{2,1,0:T(8,128)S(1)}, u32[]{:S(2)}, u32[]{:S(2)}) collective-permute-start(f32[4,128,128]{2,1,0:T(8,128)S(1)} %convolution_add_fusion.5), channel_id=1, source_target_pairs={{0,8},{8,16},{16,24},{24,32},{32,40},{40,48},{48,56},{56,64},{64,7... | collective-permute-start | bytes 786440 | tf_op jit(solution)/shard_map/while/body/eval_jaxpr/ppermute | solution.py:14
  418.6 10.5 %collective-permute-start = (f32[4,128,128]{2,1,0:T(8,128)S(1)}, f32[4,128,128]{2,1,0:T(8,128)S(1)}, u32[]{:S(2)}, u32[]{:S(2)}) collective-permute-start(f32[4,128,128]{2,1,0:T(8,128)S(1)} %convolution_add_fusion.5), channel_id=1, source_target_pairs={{0,8},{8,16},{16,24},{24,32},{32,40},{40,48},{48,56},{56,64},{64,7... | collective-permute-start | bytes 786440 | tf_op jit(solution)/shard_map/while/body/eval_jaxpr/ppermute | solution.py:14
  429.5 11.7 %collective-permute-start = (f32[4,128,128]{2,1,0:T(8,128)S(1)}, f32[4,128,128]{2,1,0:T(8,128)S(1)}, u32[]{:S(2)}, u32[]{:S(2)}) collective-permute-start(f32[4,128,128]{2,1,0:T(8,128)S(1)} %convolution_add_fusion.5), channel_id=1, source_target_pairs={{0,8},{8,16},{16,24},{24,32},{32,40},{40,48},{48,56},{56,64},{64,7... | collective-permute-start | bytes 786440 | tf_op jit(solution)/shard_map/while/body/eval_jaxpr/ppermute | solution.py:14
  441.6 12.8 %collective-permute-start = (f32[4,128,128]{2,1,0:T(8,128)S(1)}, f32[4,128,128]{2,1,0:T(8,128)S(1)}, u32[]{:S(2)}, u32[]{:S(2)}) collective-permute-start(f32[4,128,128]{2,1,0:T(8,128)S(1)} %convolution_add_fusion.5), channel_id=1, source_target_pairs={{0,8},{8,16},{16,24},{24,32},{32,40},{40,48},{48,56},{56,64},{64,7... | collective-permute-start | bytes 786440 | tf_op jit(solution)/shard_map/while/body/eval_jaxpr/ppermute | solution.py:14
  454.8 12.4 %collective-permute-start = (f32[4,128,128]{2,1,0:T(8,128)S(1)}, f32[4,128,128]{2,1,0:T(8,128)S(1)}, u32[]{:S(2)}, u32[]{:S(2)}) collective-permute-start(f32[4,128,128]{2,1,0:T(8,128)S(1)} %convolution_add_fusion.5), channel_id=1, source_target_pairs={{0,8},{8,16},{16,24},{24,32},{32,40},{40,48},{48,56},{56,64},{64,7... | collective-permute-start | bytes 786440 | tf_op jit(solution)/shard_map/while/body/eval_jaxpr/ppermute | solution.py:14
  467.6 11.6 %collective-permute-start = (f32[4,128,128]{2,1,0:T(8,128)S(1)}, f32[4,128,128]{2,1,0:T(8,128)S(1)}, u32[]{:S(2)}, u32[]{:S(2)}) collective-permute-start(f32[4,128,128]{2,1,0:T(8,128)S(1)} %convolution_add_fusion.5), channel_id=1, source_target_pairs={{0,8},{8,16},{16,24},{24,32},{32,40},{40,48},{48,56},{56,64},{64,7... | collective-permute-start | bytes 786440 | tf_op jit(solution)/shard_map/while/body/eval_jaxpr/ppermute | solution.py:14
  479.6 10.7 %collective-permute-start = (f32[4,128,128]{2,1,0:T(8,128)S(1)}, f32[4,128,128]{2,1,0:T(8,128)S(1)}, u32[]{:S(2)}, u32[]{:S(2)}) collective-permute-start(f32[4,128,128]{2,1,0:T(8,128)S(1)} %convolution_add_fusion.5), channel_id=1, source_target_pairs={{0,8},{8,16},{16,24},{24,32},{32,40},{40,48},{48,56},{56,64},{64,7... | collective-permute-start | bytes 786440 | tf_op jit(solution)/shard_map/while/body/eval_jaxpr/ppermute | solution.py:14
  490.7 10.4 %collective-permute-start = (f32[4,128,128]{2,1,0:T(8,128)S(1)}, f32[4,128,128]{2,1,0:T(8,128)S(1)}, u32[]{:S(2)}, u32[]{:S(2)}) collective-permute-start(f32[4,128,128]{2,1,0:T(8,128)S(1)} %convolution_add_fusion.5), channel_id=1, source_target_pairs={{0,8},{8,16},{16,24},{24,32},{32,40},{40,48},{48,56},{56,64},{64,7... | collective-permute-start | bytes 786440 | tf_op jit(solution)/shard_map/while/body/eval_jaxpr/ppermute | solution.py:14
  501.5 10.4 %collective-permute-start = (f32[4,128,128]{2,1,0:T(8,128)S(1)}, f32[4,128,128]{2,1,0:T(8,128)S(1)}, u32[]{:S(2)}, u32[]{:S(2)}) collective-permute-start(f32[4,128,128]{2,1,0:T(8,128)S(1)} %convolution_add_fusion.5), channel_id=1, source_target_pairs={{0,8},{8,16},{16,24},{24,32},{32,40},{40,48},{48,56},{56,64},{64,7... | collective-permute-start | bytes 786440 | tf_op jit(solution)/shard_map/while/body/eval_jaxpr/ppermute | solution.py:14
  512.3 10.4 %collective-permute-start = (f32[4,128,128]{2,1,0:T(8,128)S(1)}, f32[4,128,128]{2,1,0:T(8,128)S(1)}, u32[]{:S(2)}, u32[]{:S(2)}) collective-permute-start(f32[4,128,128]{2,1,0:T(8,128)S(1)} %convolution_add_fusion.5), channel_id=1, source_target_pairs={{0,8},{8,16},{16,24},{24,32},{32,40},{40,48},{48,56},{56,64},{64,7... | collective-permute-start | bytes 786440 | tf_op jit(solution)/shard_map/while/body/eval_jaxpr/ppermute | solution.py:14
  523.0 10.4 %collective-permute-start = (f32[4,128,128]{2,1,0:T(8,128)S(1)}, f32[4,128,128]{2,1,0:T(8,128)S(1)}, u32[]{:S(2)}, u32[]{:S(2)}) collective-permute-start(f32[4,128,128]{2,1,0:T(8,128)S(1)} %convolution_add_fusion.5), channel_id=1, source_target_pairs={{0,8},{8,16},{16,24},{24,32},{32,40},{40,48},{48,56},{56,64},{64,7... | collective-permute-start | bytes 786440 | tf_op jit(solution)/shard_map/while/body/eval_jaxpr/ppermute | solution.py:14
  533.8 11.5 %collective-permute-start = (f32[4,128,128]{2,1,0:T(8,128)S(1)}, f32[4,128,128]{2,1,0:T(8,128)S(1)}, u32[]{:S(2)}, u32[]{:S(2)}) collective-permute-start(f32[4,128,128]{2,1,0:T(8,128)S(1)} %convolution_add_fusion.5), channel_id=1, source_target_pairs={{0,8},{8,16},{16,24},{24,32},{32,40},{40,48},{48,56},{56,64},{64,7... | collective-permute-start | bytes 786440 | tf_op jit(solution)/shard_map/while/body/eval_jaxpr/ppermute | solution.py:14
  545.7 12.6 %collective-permute-start = (f32[4,128,128]{2,1,0:T(8,128)S(1)}, f32[4,128,128]{2,1,0:T(8,128)S(1)}, u32[]{:S(2)}, u32[]{:S(2)}) collective-permute-start(f32[4,128,128]{2,1,0:T(8,128)S(1)} %convolution_add_fusion.5), channel_id=1, source_target_pairs={{0,8},{8,16},{16,24},{24,32},{32,40},{40,48},{48,56},{56,64},{64,7... | collective-permute-start | bytes 786440 | tf_op jit(solution)/shard_map/while/body/eval_jaxpr/ppermute | solution.py:14
  558.8 12.6 %collective-permute-start = (f32[4,128,128]{2,1,0:T(8,128)S(1)}, f32[4,128,128]{2,1,0:T(8,128)S(1)}, u32[]{:S(2)}, u32[]{:S(2)}) collective-permute-start(f32[4,128,128]{2,1,0:T(8,128)S(1)} %convolution_add_fusion.5), channel_id=1, source_target_pairs={{0,8},{8,16},{16,24},{24,32},{32,40},{40,48},{48,56},{56,64},{64,7... | collective-permute-start | bytes 786440 | tf_op jit(solution)/shard_map/while/body/eval_jaxpr/ppermute | solution.py:14
  571.8 11.7 %collective-permute-start = (f32[4,128,128]{2,1,0:T(8,128)S(1)}, f32[4,128,128]{2,1,0:T(8,128)S(1)}, u32[]{:S(2)}, u32[]{:S(2)}) collective-permute-start(f32[4,128,128]{2,1,0:T(8,128)S(1)} %convolution_add_fusion.5), channel_id=1, source_target_pairs={{0,8},{8,16},{16,24},{24,32},{32,40},{40,48},{48,56},{56,64},{64,7... | collective-permute-start | bytes 786440 | tf_op jit(solution)/shard_map/while/body/eval_jaxpr/ppermute | solution.py:14
  583.9 10.4 %collective-permute-start = (f32[4,128,128]{2,1,0:T(8,128)S(1)}, f32[4,128,128]{2,1,0:T(8,128)S(1)}, u32[]{:S(2)}, u32[]{:S(2)}) collective-permute-start(f32[4,128,128]{2,1,0:T(8,128)S(1)} %convolution_add_fusion.5), channel_id=1, source_target_pairs={{0,8},{8,16},{16,24},{24,32},{32,40},{40,48},{48,56},{56,64},{64,7... | collective-permute-start | bytes 786440 | tf_op jit(solution)/shard_map/while/body/eval_jaxpr/ppermute | solution.py:14
  (7 other events, 205.7 us)
where the time goes:
time: 660 us; the launch traced here: 657 us
  waiting for transfers between devices  281 us (43%)
  other arithmetic  169 us (26%)
  matrix products  101 us (15%)
  starting transfers between devices  75.1 us (11%)
  blocking collectives  14.6 us (2%)
  local copies, waits for them, and re-layouts  14.4 us (2%)
    ppermute x34, waiting for transfers between devices, shifted(): lax.ppermute(value, axis, [(source, source + steps) for source in range(f...  281 us
    another operation x3, other arithmetic, group_terms(): lax.linalg.triangular_solve(identity_mats + strict, identity_mats, left_s...  157 us
    ppermute x34, starting transfers between devices, shifted(): lax.ppermute(value, axis, [(source, source + steps) for source in range(f...  75.1 us
    dot_general x56, matrix products, matmul_pair(): jnp.einsum('...ij,...jk->...ik', left_mats, right_mats, precision=highest)  46.4 us
    all_to_all x1, blocking collectives, body(): lax.all_to_all(normed, 'head', split_axis=0, concat_axis=1, tiled=True)  14.6 us
  transfers between devices with their start and end apart: 34, of which 31 were waited for; matrix products, arithmetic and copies ran while one was open for 28% of the time, Pallas kernels for 0%

commit v1 on v0

--- a/solution.py
+++ b/solution.py
@@ -159,7 +159,10 @@
         * jax.nn.silu(gates)
     )
     normed = normed.astype(jnp.bfloat16).reshape(length, value_heads * head_size)
-    return lax.all_to_all(normed, "head", split_axis=0, concat_axis=1, tiled=True)
+    roots_recast = lambda my_data: jnp.concatenate(
+        lax.all_to_all(jnp.stack(jnp.split(my_data, lax.axis_size("head"), 0), 0), "head", 0, 0), 1
+    )
+    return roots_recast(normed)
 
 
 def solution(mesh):

time: 660 us -> 660 us (level)
  no operation moved by 1% of the time
where the time goes in v1:
time: 660 us; the launch traced here: 658 us
  waiting for transfers between devices  281 us (43%)
  other arithmetic  169 us (26%)
  matrix products  100 us (15%)
  starting transfers between devices  75.1 us (11%)
  local copies, waits for them, and re-layouts  15.2 us (2%)
  blocking collectives  14.6 us (2%)
    ppermute x34, waiting for transfers between devices, shifted(): lax.ppermute(value, axis, [(source, source + steps) for source in range(f...  281 us
    another operation x3, other arithmetic, group_terms(): lax.linalg.triangular_solve(identity_mats + strict, identity_mats, left_s...  157 us
    ppermute x34, starting transfers between devices, shifted(): lax.ppermute(value, axis, [(source, source + steps) for source in range(f...  75.1 us
    dot_general x56, matrix products, matmul_pair(): jnp.einsum('...ij,...jk->...ik', left_mats, right_mats, precision=highest)  46.1 us
    all_to_all x1, blocking collectives, body(): lax.all_to_all(jnp.stack(jnp.split(my_data, lax.axis_size('head'), 0), 0)...  14.6 us
  transfers between devices with their start and end apart: 34, of which 31 were waited for; matrix products, arithmetic and copies ran while one was open for 28% of the time, Pallas kernels for 0%

profile of v1, /device:TPU:2, one launch (start us, length us, event | category | flops | bytes accessed | tf_op | source)
XLA Modules:
  0.0 657.7 jit_solution(15784304352971215489)
XLA Ops:
  24.5 157.3 %custom-call.3 = f32[8,4,1,64,64]{3,4,2,1,0:T(8,128)S(1)} custom-call(f32[8,4,1,64,64]{4,3,2,1,0:T(8,128)S(1)} %fusion.42), custom_call_target="InvertDiagBlocksLowerTriangular" | custom-call | tf_op jit(solution)/shard_map/triangular_solve | solution.py:39
  205.9 53.2 %while.39 = (s32[]{:T(128)}, f32[4,128,128]{2,1,0:T(8,128)S(1)}, f32[4,128,128]{2,1,0:T(8,128)S(1)}, f32[8,4,64,128]{3,2,0,1:T(8,128)S(1)}, f32[8,4]{1,0:T(8,128...) while((s32[]{:T(128)}, f32[4,128,128]{2,1,0:T(8,128)S(1)}, ...), condition=%wide.region_4.5_spmd.clone, body=%wide.region_3.4_spmd.clone.sunk | while | flops 277217280 | bytes 3804367 | solution.py:139
  259.2 357.5 %while.37 = (s32[]{:T(128)}, f32[4,128,128]{2,1,0:T(8,128)S(1)}, f32[4,128,128]{2,1,0:T(8,128)S(1)}, f32[4,128,128]{2,1,0:T(8,128)S(1)}, s32[]{:T(128)}) while((s32[]{:T(128)}, f32[4,128,128]{2,1,0:T(8,128)S(1)}, f32[4,128,128]{2,1,0:T(8,128)S(1)}, f32[4,128,128]{2,1,0:T(8,128)S(1)}, s32[]{:T(128)}) %tuple.77), condition=%wide.region_6.7_spmd, body=%wide.region_5.6_spmd.sunk | while | flops 100728832 | bytes 2097253 | solution.py:146
  284.1 8.4 %collective-permute-done = f32[4,128,128]{2,1,0:T(8,128)S(1)} collective-permute-done((f32[4,128,128]{2,1,0:T(8,128)S(1)}, f32[4,128,128]{2,1,0:T(8,128)S(1)}, u32[]{:S(2)}, u32[]{:S(2)}) %collective-permute-start) | collective-permute-done | bytes 262176 | tf_op jit(solution)/shard_map/while/body/eval_jaxpr/ppermute | solution.py:14
  294.9 8.4 %collective-permute-done = f32[4,128,128]{2,1,0:T(8,128)S(1)} collective-permute-done((f32[4,128,128]{2,1,0:T(8,128)S(1)}, f32[4,128,128]{2,1,0:T(8,128)S(1)}, u32[]{:S(2)}, u32[]{:S(2)}) %collective-permute-start) | collective-permute-done | bytes 262176 | tf_op jit(solution)/shard_map/while/body/eval_jaxpr/ppermute | solution.py:14
  305.7 8.4 %collective-permute-done = f32[4,128,128]{2,1,0:T(8,128)S(1)} collective-permute-done((f32[4,128,128]{2,1,0:T(8,128)S(1)}, f32[4,128,128]{2,1,0:T(8,128)S(1)}, u32[]{:S(2)}, u32[]{:S(2)}) %collective-permute-start) | collective-permute-done | bytes 262176 | tf_op jit(solution)/shard_map/while/body/eval_jaxpr/ppermute | solution.py:14
  316.5 9.1 %collective-permute-done = f32[4,128,128]{2,1,0:T(8,128)S(1)} collective-permute-done((f32[4,128,128]{2,1,0:T(8,128)S(1)}, f32[4,128,128]{2,1,0:T(8,128)S(1)}, u32[]{:S(2)}, u32[]{:S(2)}) %collective-permute-start) | collective-permute-done | bytes 262176 | tf_op jit(solution)/shard_map/while/body/eval_jaxpr/ppermute | solution.py:14
  327.9 10.2 %collective-permute-done = f32[4,128,128]{2,1,0:T(8,128)S(1)} collective-permute-done((f32[4,128,128]{2,1,0:T(8,128)S(1)}, f32[4,128,128]{2,1,0:T(8,128)S(1)}, u32[]{:S(2)}, u32[]{:S(2)}) %collective-permute-start) | collective-permute-done | bytes 262176 | tf_op jit(solution)/shard_map/while/body/eval_jaxpr/ppermute | solution.py:14
  340.4 11.2 %collective-permute-done = f32[4,128,128]{2,1,0:T(8,128)S(1)} collective-permute-done((f32[4,128,128]{2,1,0:T(8,128)S(1)}, f32[4,128,128]{2,1,0:T(8,128)S(1)}, u32[]{:S(2)}, u32[]{:S(2)}) %collective-permute-start) | collective-permute-done | bytes 262176 | tf_op jit(solution)/shard_map/while/body/eval_jaxpr/ppermute | solution.py:14
  353.9 10.3 %collective-permute-done = f32[4,128,128]{2,1,0:T(8,128)S(1)} collective-permute-done((f32[4,128,128]{2,1,0:T(8,128)S(1)}, f32[4,128,128]{2,1,0:T(8,128)S(1)}, u32[]{:S(2)}, u32[]{:S(2)}) %collective-permute-start) | collective-permute-done | bytes 262176 | tf_op jit(solution)/shard_map/while/body/eval_jaxpr/ppermute | solution.py:14
  366.5 9.4 %collective-permute-done = f32[4,128,128]{2,1,0:T(8,128)S(1)} collective-permute-done((f32[4,128,128]{2,1,0:T(8,128)S(1)}, f32[4,128,128]{2,1,0:T(8,128)S(1)}, u32[]{:S(2)}, u32[]{:S(2)}) %collective-permute-start) | collective-permute-done | bytes 262176 | tf_op jit(solution)/shard_map/while/body/eval_jaxpr/ppermute | solution.py:14
  378.3 8.6 %collective-permute-done = f32[4,128,128]{2,1,0:T(8,128)S(1)} collective-permute-done((f32[4,128,128]{2,1,0:T(8,128)S(1)}, f32[4,128,128]{2,1,0:T(8,128)S(1)}, u32[]{:S(2)}, u32[]{:S(2)}) %collective-permute-start) | collective-permute-done | bytes 262176 | tf_op jit(solution)/shard_map/while/body/eval_jaxpr/ppermute | solution.py:14
  389.2 8.4 %collective-permute-done = f32[4,128,128]{2,1,0:T(8,128)S(1)} collective-permute-done((f32[4,128,128]{2,1,0:T(8,128)S(1)}, f32[4,128,128]{2,1,0:T(8,128)S(1)}, u32[]{:S(2)}, u32[]{:S(2)}) %collective-permute-start) | collective-permute-done | bytes 262176 | tf_op jit(solution)/shard_map/while/body/eval_jaxpr/ppermute | solution.py:14
  400.0 8.4 %collective-permute-done = f32[4,128,128]{2,1,0:T(8,128)S(1)} collective-permute-done((f32[4,128,128]{2,1,0:T(8,128)S(1)}, f32[4,128,128]{2,1,0:T(8,128)S(1)}, u32[]{:S(2)}, u32[]{:S(2)}) %collective-permute-start) | collective-permute-done | bytes 262176 | tf_op jit(solution)/shard_map/while/body/eval_jaxpr/ppermute | solution.py:14
  410.7 8.4 %collective-permute-done = f32[4,128,128]{2,1,0:T(8,128)S(1)} collective-permute-done((f32[4,128,128]{2,1,0:T(8,128)S(1)}, f32[4,128,128]{2,1,0:T(8,128)S(1)}, u32[]{:S(2)}, u32[]{:S(2)}) %collective-permute-start) | collective-permute-done | bytes 262176 | tf_op jit(solution)/shard_map/while/body/eval_jaxpr/ppermute | solution.py:14
  421.5 8.6 %collective-permute-done = f32[4,128,128]{2,1,0:T(8,128)S(1)} collective-permute-done((f32[4,128,128]{2,1,0:T(8,128)S(1)}, f32[4,128,128]{2,1,0:T(8,128)S(1)}, u32[]{:S(2)}, u32[]{:S(2)}) %collective-permute-start) | collective-permute-done | bytes 262176 | tf_op jit(solution)/shard_map/while/body/eval_jaxpr/ppermute | solution.py:14
  432.4 9.7 %collective-permute-done = f32[4,128,128]{2,1,0:T(8,128)S(1)} collective-permute-done((f32[4,128,128]{2,1,0:T(8,128)S(1)}, f32[4,128,128]{2,1,0:T(8,128)S(1)}, u32[]{:S(2)}, u32[]{:S(2)}) %collective-permute-start) | collective-permute-done | bytes 262176 | tf_op jit(solution)/shard_map/while/body/eval_jaxpr/ppermute | solution.py:14
  444.5 10.9 %collective-permute-done = f32[4,128,128]{2,1,0:T(8,128)S(1)} collective-permute-done((f32[4,128,128]{2,1,0:T(8,128)S(1)}, f32[4,128,128]{2,1,0:T(8,128)S(1)}, u32[]{:S(2)}, u32[]{:S(2)}) %collective-permute-start) | collective-permute-done | bytes 262176 | tf_op jit(solution)/shard_map/while/body/eval_jaxpr/ppermute | solution.py:14
  457.7 10.5 %collective-permute-done = f32[4,128,128]{2,1,0:T(8,128)S(1)} collective-permute-done((f32[4,128,128]{2,1,0:T(8,128)S(1)}, f32[4,128,128]{2,1,0:T(8,128)S(1)}, u32[]{:S(2)}, u32[]{:S(2)}) %collective-permute-start) | collective-permute-done | bytes 262176 | tf_op jit(solution)/shard_map/while/body/eval_jaxpr/ppermute | solution.py:14
  470.5 9.6 %collective-permute-done = f32[4,128,128]{2,1,0:T(8,128)S(1)} collective-permute-done((f32[4,128,128]{2,1,0:T(8,128)S(1)}, f32[4,128,128]{2,1,0:T(8,128)S(1)}, u32[]{:S(2)}, u32[]{:S(2)}) %collective-permute-start) | collective-permute-done | bytes 262176 | tf_op jit(solution)/shard_map/while/body/eval_jaxpr/ppermute | solution.py:14
  482.5 8.8 %collective-permute-done = f32[4,128,128]{2,1,0:T(8,128)S(1)} collective-permute-done((f32[4,128,128]{2,1,0:T(8,128)S(1)}, f32[4,128,128]{2,1,0:T(8,128)S(1)}, u32[]{:S(2)}, u32[]{:S(2)}) %collective-permute-start) | collective-permute-done | bytes 262176 | tf_op jit(solution)/shard_map/while/body/eval_jaxpr/ppermute | solution.py:14
  493.6 8.4 %collective-permute-done = f32[4,128,128]{2,1,0:T(8,128)S(1)} collective-permute-done((f32[4,128,128]{2,1,0:T(8,128)S(1)}, f32[4,128,128]{2,1,0:T(8,128)S(1)}, u32[]{:S(2)}, u32[]{:S(2)}) %collective-permute-start) | collective-permute-done | bytes 262176 | tf_op jit(solution)/shard_map/while/body/eval_jaxpr/ppermute | solution.py:14
  504.3 8.4 %collective-permute-done = f32[4,128,128]{2,1,0:T(8,128)S(1)} collective-permute-done((f32[4,128,128]{2,1,0:T(8,128)S(1)}, f32[4,128,128]{2,1,0:T(8,128)S(1)}, u32[]{:S(2)}, u32[]{:S(2)}) %collective-permute-start) | collective-permute-done | bytes 262176 | tf_op jit(solution)/shard_map/while/body/eval_jaxpr/ppermute | solution.py:14
  525.9 8.4 %collective-permute-done = f32[4,128,128]{2,1,0:T(8,128)S(1)} collective-permute-done((f32[4,128,128]{2,1,0:T(8,128)S(1)}, f32[4,128,128]{2,1,0:T(8,128)S(1)}, u32[]{:S(2)}, u32[]{:S(2)}) %collective-permute-start) | collective-permute-done | bytes 262176 | tf_op jit(solution)/shard_map/while/body/eval_jaxpr/ppermute | solution.py:14
  536.7 9.6 %collective-permute-done = f32[4,128,128]{2,1,0:T(8,128)S(1)} collective-permute-done((f32[4,128,128]{2,1,0:T(8,128)S(1)}, f32[4,128,128]{2,1,0:T(8,128)S(1)}, u32[]{:S(2)}, u32[]{:S(2)}) %collective-permute-start) | collective-permute-done | bytes 262176 | tf_op jit(solution)/shard_map/while/body/eval_jaxpr/ppermute | solution.py:14
  548.6 10.7 %collective-permute-done = f32[4,128,128]{2,1,0:T(8,128)S(1)} collective-permute-done((f32[4,128,128]{2,1,0:T(8,128)S(1)}, f32[4,128,128]{2,1,0:T(8,128)S(1)}, u32[]{:S(2)}, u32[]{:S(2)}) %collective-permute-start) | collective-permute-done | bytes 262176 | tf_op jit(solution)/shard_map/while/body/eval_jaxpr/ppermute | solution.py:14
  561.6 10.6 %collective-permute-done = f32[4,128,128]{2,1,0:T(8,128)S(1)} collective-permute-done((f32[4,128,128]{2,1,0:T(8,128)S(1)}, f32[4,128,128]{2,1,0:T(8,128)S(1)}, u32[]{:S(2)}, u32[]{:S(2)}) %collective-permute-start) | collective-permute-done | bytes 262176 | tf_op jit(solution)/shard_map/while/body/eval_jaxpr/ppermute | solution.py:14
  574.6 9.8 %collective-permute-done = f32[4,128,128]{2,1,0:T(8,128)S(1)} collective-permute-done((f32[4,128,128]{2,1,0:T(8,128)S(1)}, f32[4,128,128]{2,1,0:T(8,128)S(1)}, u32[]{:S(2)}, u32[]{:S(2)}) %collective-permute-start) | collective-permute-done | bytes 262176 | tf_op jit(solution)/shard_map/while/body/eval_jaxpr/ppermute | solution.py:14
  586.7 8.4 %collective-permute-done = f32[4,128,128]{2,1,0:T(8,128)S(1)} collective-permute-done((f32[4,128,128]{2,1,0:T(8,128)S(1)}, f32[4,128,128]{2,1,0:T(8,128)S(1)}, u32[]{:S(2)}, u32[]{:S(2)}) %collective-permute-start) | collective-permute-done | bytes 262176 | tf_op jit(solution)/shard_map/while/body/eval_jaxpr/ppermute | solution.py:14
  608.3 8.4 %collective-permute-done = f32[4,128,128]{2,1,0:T(8,128)S(1)} collective-permute-done((f32[4,128,128]{2,1,0:T(8,128)S(1)}, f32[4,128,128]{2,1,0:T(8,128)S(1)}, u32[]{:S(2)}, u32[]{:S(2)}) %collective-permute-start) | collective-permute-done | bytes 262176 | tf_op jit(solution)/shard_map/while/body/eval_jaxpr/ppermute | solution.py:14
  616.8 21.3 %while.38 = (s32[]{:T(128)}, f32[4,128,128]{2,1,0:T(8,128)S(1)}, f32[8,4,64,128]{3,2,0,1:T(8,128)S(1)}, f32[8,4,128,128]{3,2,1,0:T(8,128)}, f32[8,4,64,128]{3,2,1,0:T(8,128)}, /*index=5*/s32[]{:T(128)}) while((s32[]{:T(128)}, f32[4,128,128]{2,1,0:T(8,128)S(1)}, f32[8,4,64,128]{3,2,0,1:T(8,128)S(1)}, f32[8,4,128,128]{3,2,1,0:T(8,128)}, ...), condition=%wide.region_8.9_spmd, body=%wide.region_7.8_spmd.sunk | while | flops 150994944 | bytes 1836113 | solution.py:152
  642.3 14.6 %all_to_all.5 = bf16[8,64,512]{2,1,0:T(8,128)(2,1)S(1)} all-to-all(bf16[8,64,512]{2,1,0:T(8,128)(2,1)S(1)} %constant_dynamic-update-slice_fusion), channel_id=1, replica_groups=mesh['ctx'=32,'head'=8] {'head'}, dimensions={0} | all-to-all | bytes 1048576 | tf_op jit(solution)/shard_map/all_to_all | solution.py:163
  (248 shorter events, 233.3 us)
Async XLA Ops:
  0.8 20.9 %collective-permute-start.1 = (bf16[3,256]{1,0:T(4,128)(2,1)S(1)}, bf16[3,256]{1,0:T(4,128)(2,1)S(1)}, u32[]{:S(2)}, u32[]{:S(2)}) collective-permute-start(bf16[3,256]{1,0:T(4,128)(2,1)S(1)} %slice.89), channel_id=1, source_target_pairs={{0,8},{8,16},{16,24},{24,32},{32,40},{40,48},{48,56},{56,64},{64,7... | collective-permute-start | bytes 4616 | tf_op jit(solution)/shard_map/ppermute | solution.py:14
  5.3 192.8 %collective-permute-start.2 = (bf16[3,512]{1,0:T(4,128)(2,1)S(1)}, bf16[3,512]{1,0:T(4,128)(2,1)S(1)}, u32[]{:S(2)}, u32[]{:S(2)}) collective-permute-start(bf16[3,512]{1,0:T(4,128)(2,1)S(1)} %slice.97), channel_id=1, source_target_pairs={{0,8},{8,16},{16,24},{24,32},{32,40},{40,48},{48,56},{56,64},{64,7... | collective-permute-start | bytes 9224 | tf_op jit(solution)/shard_map/ppermute | solution.py:14
  9.8 173.8 %collective-permute-start.3 = (bf16[3,256]{1,0:T(4,128)(2,1)S(1)}, bf16[3,256]{1,0:T(4,128)(2,1)S(1)}, u32[]{:S(2)}, u32[]{:S(2)}) collective-permute-start(bf16[3,256]{1,0:T(4,128)(2,1)S(1)} %slice.105), channel_id=1, source_target_pairs={{0,8},{8,16},{16,24},{24,32},{32,40},{40,48},{48,56},{56,64},{64,7... | collective-permute-start | bytes 4616 | tf_op jit(solution)/shard_map/ppermute | solution.py:14
  259.8 11.2 %collective-permute-start = (f32[4,128,128]{2,1,0:T(8,128)S(1)}, f32[4,128,128]{2,1,0:T(8,128)S(1)}, u32[]{:S(2)}, u32[]{:S(2)}) collective-permute-start(f32[4,128,128]{2,1,0:T(8,128)S(1)} %convolution_add_fusion.5), channel_id=1, source_target_pairs={{0,8},{8,16},{16,24},{24,32},{32,40},{40,48},{48,56},{56,64},{64,7... | collective-permute-start | bytes 786440 | tf_op jit(solution)/shard_map/while/body/eval_jaxpr/ppermute | solution.py:14
  271.4 10.4 %collective-permute-start = (f32[4,128,128]{2,1,0:T(8,128)S(1)}, f32[4,128,128]{2,1,0:T(8,128)S(1)}, u32[]{:S(2)}, u32[]{:S(2)}) collective-permute-start(f32[4,128,128]{2,1,0:T(8,128)S(1)} %convolution_add_fusion.5), channel_id=1, source_target_pairs={{0,8},{8,16},{16,24},{24,32},{32,40},{40,48},{48,56},{56,64},{64,7... | collective-permute-start | bytes 786440 | tf_op jit(solution)/shard_map/while/body/eval_jaxpr/ppermute | solution.py:14
  282.2 10.4 %collective-permute-start = (f32[4,128,128]{2,1,0:T(8,128)S(1)}, f32[4,128,128]{2,1,0:T(8,128)S(1)}, u32[]{:S(2)}, u32[]{:S(2)}) collective-permute-start(f32[4,128,128]{2,1,0:T(8,128)S(1)} %convolution_add_fusion.5), channel_id=1, source_target_pairs={{0,8},{8,16},{16,24},{24,32},{32,40},{40,48},{48,56},{56,64},{64,7... | collective-permute-start | bytes 786440 | tf_op jit(solution)/shard_map/while/body/eval_jaxpr/ppermute | solution.py:14
  293.0 10.4 %collective-permute-start = (f32[4,128,128]{2,1,0:T(8,128)S(1)}, f32[4,128,128]{2,1,0:T(8,128)S(1)}, u32[]{:S(2)}, u32[]{:S(2)}) collective-permute-start(f32[4,128,128]{2,1,0:T(8,128)S(1)} %convolution_add_fusion.5), channel_id=1, source_target_pairs={{0,8},{8,16},{16,24},{24,32},{32,40},{40,48},{48,56},{56,64},{64,7... | collective-permute-start | bytes 786440 | tf_op jit(solution)/shard_map/while/body/eval_jaxpr/ppermute | solution.py:14
  303.8 10.4 %collective-permute-start = (f32[4,128,128]{2,1,0:T(8,128)S(1)}, f32[4,128,128]{2,1,0:T(8,128)S(1)}, u32[]{:S(2)}, u32[]{:S(2)}) collective-permute-start(f32[4,128,128]{2,1,0:T(8,128)S(1)} %convolution_add_fusion.5), channel_id=1, source_target_pairs={{0,8},{8,16},{16,24},{24,32},{32,40},{40,48},{48,56},{56,64},{64,7... | collective-permute-start | bytes 786440 | tf_op jit(solution)/shard_map/while/body/eval_jaxpr/ppermute | solution.py:14
  314.5 11.0 %collective-permute-start = (f32[4,128,128]{2,1,0:T(8,128)S(1)}, f32[4,128,128]{2,1,0:T(8,128)S(1)}, u32[]{:S(2)}, u32[]{:S(2)}) collective-permute-start(f32[4,128,128]{2,1,0:T(8,128)S(1)} %convolution_add_fusion.5), channel_id=1, source_target_pairs={{0,8},{8,16},{16,24},{24,32},{32,40},{40,48},{48,56},{56,64},{64,7... | collective-permute-start | bytes 786440 | tf_op jit(solution)/shard_map/while/body/eval_jaxpr/ppermute | solution.py:14
  325.9 12.1 %collective-permute-start = (f32[4,128,128]{2,1,0:T(8,128)S(1)}, f32[4,128,128]{2,1,0:T(8,128)S(1)}, u32[]{:S(2)}, u32[]{:S(2)}) collective-permute-start(f32[4,128,128]{2,1,0:T(8,128)S(1)} %convolution_add_fusion.5), channel_id=1, source_target_pairs={{0,8},{8,16},{16,24},{24,32},{32,40},{40,48},{48,56},{56,64},{64,7... | collective-permute-start | bytes 786440 | tf_op jit(solution)/shard_map/while/body/eval_jaxpr/ppermute | solution.py:14
  338.5 13.1 %collective-permute-start = (f32[4,128,128]{2,1,0:T(8,128)S(1)}, f32[4,128,128]{2,1,0:T(8,128)S(1)}, u32[]{:S(2)}, u32[]{:S(2)}) collective-permute-start(f32[4,128,128]{2,1,0:T(8,128)S(1)} %convolution_add_fusion.5), channel_id=1, source_target_pairs={{0,8},{8,16},{16,24},{24,32},{32,40},{40,48},{48,56},{56,64},{64,7... | collective-permute-start | bytes 786440 | tf_op jit(solution)/shard_map/while/body/eval_jaxpr/ppermute | solution.py:14
  352.0 12.2 %collective-permute-start = (f32[4,128,128]{2,1,0:T(8,128)S(1)}, f32[4,128,128]{2,1,0:T(8,128)S(1)}, u32[]{:S(2)}, u32[]{:S(2)}) collective-permute-start(f32[4,128,128]{2,1,0:T(8,128)S(1)} %convolution_add_fusion.5), channel_id=1, source_target_pairs={{0,8},{8,16},{16,24},{24,32},{32,40},{40,48},{48,56},{56,64},{64,7... | collective-permute-start | bytes 786440 | tf_op jit(solution)/shard_map/while/body/eval_jaxpr/ppermute | solution.py:14
  364.6 11.4 %collective-permute-start = (f32[4,128,128]{2,1,0:T(8,128)S(1)}, f32[4,128,128]{2,1,0:T(8,128)S(1)}, u32[]{:S(2)}, u32[]{:S(2)}) collective-permute-start(f32[4,128,128]{2,1,0:T(8,128)S(1)} %convolution_add_fusion.5), channel_id=1, source_target_pairs={{0,8},{8,16},{16,24},{24,32},{32,40},{40,48},{48,56},{56,64},{64,7... | collective-permute-start | bytes 786440 | tf_op jit(solution)/shard_map/while/body/eval_jaxpr/ppermute | solution.py:14
  376.3 10.5 %collective-permute-start = (f32[4,128,128]{2,1,0:T(8,128)S(1)}, f32[4,128,128]{2,1,0:T(8,128)S(1)}, u32[]{:S(2)}, u32[]{:S(2)}) collective-permute-start(f32[4,128,128]{2,1,0:T(8,128)S(1)} %convolution_add_fusion.5), channel_id=1, source_target_pairs={{0,8},{8,16},{16,24},{24,32},{32,40},{40,48},{48,56},{56,64},{64,7... | collective-permute-start | bytes 786440 | tf_op jit(solution)/shard_map/while/body/eval_jaxpr/ppermute | solution.py:14
  387.3 10.4 %collective-permute-start = (f32[4,128,128]{2,1,0:T(8,128)S(1)}, f32[4,128,128]{2,1,0:T(8,128)S(1)}, u32[]{:S(2)}, u32[]{:S(2)}) collective-permute-start(f32[4,128,128]{2,1,0:T(8,128)S(1)} %convolution_add_fusion.5), channel_id=1, source_target_pairs={{0,8},{8,16},{16,24},{24,32},{32,40},{40,48},{48,56},{56,64},{64,7... | collective-permute-start | bytes 786440 | tf_op jit(solution)/shard_map/while/body/eval_jaxpr/ppermute | solution.py:14
  398.0 10.4 %collective-permute-start = (f32[4,128,128]{2,1,0:T(8,128)S(1)}, f32[4,128,128]{2,1,0:T(8,128)S(1)}, u32[]{:S(2)}, u32[]{:S(2)}) collective-permute-start(f32[4,128,128]{2,1,0:T(8,128)S(1)} %convolution_add_fusion.5), channel_id=1, source_target_pairs={{0,8},{8,16},{16,24},{24,32},{32,40},{40,48},{48,56},{56,64},{64,7... | collective-permute-start | bytes 786440 | tf_op jit(solution)/shard_map/while/body/eval_jaxpr/ppermute | solution.py:14
  408.8 10.4 %collective-permute-start = (f32[4,128,128]{2,1,0:T(8,128)S(1)}, f32[4,128,128]{2,1,0:T(8,128)S(1)}, u32[]{:S(2)}, u32[]{:S(2)}) collective-permute-start(f32[4,128,128]{2,1,0:T(8,128)S(1)} %convolution_add_fusion.5), channel_id=1, source_target_pairs={{0,8},{8,16},{16,24},{24,32},{32,40},{40,48},{48,56},{56,64},{64,7... | collective-permute-start | bytes 786440 | tf_op jit(solution)/shard_map/while/body/eval_jaxpr/ppermute | solution.py:14
  419.6 10.5 %collective-permute-start = (f32[4,128,128]{2,1,0:T(8,128)S(1)}, f32[4,128,128]{2,1,0:T(8,128)S(1)}, u32[]{:S(2)}, u32[]{:S(2)}) collective-permute-start(f32[4,128,128]{2,1,0:T(8,128)S(1)} %convolution_add_fusion.5), channel_id=1, source_target_pairs={{0,8},{8,16},{16,24},{24,32},{32,40},{40,48},{48,56},{56,64},{64,7... | collective-permute-start | bytes 786440 | tf_op jit(solution)/shard_map/while/body/eval_jaxpr/ppermute | solution.py:14
  430.5 11.7 %collective-permute-start = (f32[4,128,128]{2,1,0:T(8,128)S(1)}, f32[4,128,128]{2,1,0:T(8,128)S(1)}, u32[]{:S(2)}, u32[]{:S(2)}) collective-permute-start(f32[4,128,128]{2,1,0:T(8,128)S(1)} %convolution_add_fusion.5), channel_id=1, source_target_pairs={{0,8},{8,16},{16,24},{24,32},{32,40},{40,48},{48,56},{56,64},{64,7... | collective-permute-start | bytes 786440 | tf_op jit(solution)/shard_map/while/body/eval_jaxpr/ppermute | solution.py:14
  442.6 12.8 %collective-permute-start = (f32[4,128,128]{2,1,0:T(8,128)S(1)}, f32[4,128,128]{2,1,0:T(8,128)S(1)}, u32[]{:S(2)}, u32[]{:S(2)}) collective-permute-start(f32[4,128,128]{2,1,0:T(8,128)S(1)} %convolution_add_fusion.5), channel_id=1, source_target_pairs={{0,8},{8,16},{16,24},{24,32},{32,40},{40,48},{48,56},{56,64},{64,7... | collective-permute-start | bytes 786440 | tf_op jit(solution)/shard_map/while/body/eval_jaxpr/ppermute | solution.py:14
  455.8 12.4 %collective-permute-start = (f32[4,128,128]{2,1,0:T(8,128)S(1)}, f32[4,128,128]{2,1,0:T(8,128)S(1)}, u32[]{:S(2)}, u32[]{:S(2)}) collective-permute-start(f32[4,128,128]{2,1,0:T(8,128)S(1)} %convolution_add_fusion.5), channel_id=1, source_target_pairs={{0,8},{8,16},{16,24},{24,32},{32,40},{40,48},{48,56},{56,64},{64,7... | collective-permute-start | bytes 786440 | tf_op jit(solution)/shard_map/while/body/eval_jaxpr/ppermute | solution.py:14
  468.6 11.5 %collective-permute-start = (f32[4,128,128]{2,1,0:T(8,128)S(1)}, f32[4,128,128]{2,1,0:T(8,128)S(1)}, u32[]{:S(2)}, u32[]{:S(2)}) collective-permute-start(f32[4,128,128]{2,1,0:T(8,128)S(1)} %convolution_add_fusion.5), channel_id=1, source_target_pairs={{0,8},{8,16},{16,24},{24,32},{32,40},{40,48},{48,56},{56,64},{64,7... | collective-permute-start | bytes 786440 | tf_op jit(solution)/shard_map/while/body/eval_jaxpr/ppermute | solution.py:14
  480.5 10.7 %collective-permute-start = (f32[4,128,128]{2,1,0:T(8,128)S(1)}, f32[4,128,128]{2,1,0:T(8,128)S(1)}, u32[]{:S(2)}, u32[]{:S(2)}) collective-permute-start(f32[4,128,128]{2,1,0:T(8,128)S(1)} %convolution_add_fusion.5), channel_id=1, source_target_pairs={{0,8},{8,16},{16,24},{24,32},{32,40},{40,48},{48,56},{56,64},{64,7... | collective-permute-start | bytes 786440 | tf_op jit(solution)/shard_map/while/body/eval_jaxpr/ppermute | solution.py:14
  491.6 10.4 %collective-permute-start = (f32[4,128,128]{2,1,0:T(8,128)S(1)}, f32[4,128,128]{2,1,0:T(8,128)S(1)}, u32[]{:S(2)}, u32[]{:S(2)}) collective-permute-start(f32[4,128,128]{2,1,0:T(8,128)S(1)} %convolution_add_fusion.5), channel_id=1, source_target_pairs={{0,8},{8,16},{16,24},{24,32},{32,40},{40,48},{48,56},{56,64},{64,7... | collective-permute-start | bytes 786440 | tf_op jit(solution)/shard_map/while/body/eval_jaxpr/ppermute | solution.py:14
  502.4 10.4 %collective-permute-start = (f32[4,128,128]{2,1,0:T(8,128)S(1)}, f32[4,128,128]{2,1,0:T(8,128)S(1)}, u32[]{:S(2)}, u32[]{:S(2)}) collective-permute-start(f32[4,128,128]{2,1,0:T(8,128)S(1)} %convolution_add_fusion.5), channel_id=1, source_target_pairs={{0,8},{8,16},{16,24},{24,32},{32,40},{40,48},{48,56},{56,64},{64,7... | collective-permute-start | bytes 786440 | tf_op jit(solution)/shard_map/while/body/eval_jaxpr/ppermute | solution.py:14
  513.2 10.4 %collective-permute-start = (f32[4,128,128]{2,1,0:T(8,128)S(1)}, f32[4,128,128]{2,1,0:T(8,128)S(1)}, u32[]{:S(2)}, u32[]{:S(2)}) collective-permute-start(f32[4,128,128]{2,1,0:T(8,128)S(1)} %convolution_add_fusion.5), channel_id=1, source_target_pairs={{0,8},{8,16},{16,24},{24,32},{32,40},{40,48},{48,56},{56,64},{64,7... | collective-permute-start | bytes 786440 | tf_op jit(solution)/shard_map/while/body/eval_jaxpr/ppermute | solution.py:14
  524.0 10.4 %collective-permute-start = (f32[4,128,128]{2,1,0:T(8,128)S(1)}, f32[4,128,128]{2,1,0:T(8,128)S(1)}, u32[]{:S(2)}, u32[]{:S(2)}) collective-permute-start(f32[4,128,128]{2,1,0:T(8,128)S(1)} %convolution_add_fusion.5), channel_id=1, source_target_pairs={{0,8},{8,16},{16,24},{24,32},{32,40},{40,48},{48,56},{56,64},{64,7... | collective-permute-start | bytes 786440 | tf_op jit(solution)/shard_map/while/body/eval_jaxpr/ppermute | solution.py:14
  534.7 11.5 %collective-permute-start = (f32[4,128,128]{2,1,0:T(8,128)S(1)}, f32[4,128,128]{2,1,0:T(8,128)S(1)}, u32[]{:S(2)}, u32[]{:S(2)}) collective-permute-start(f32[4,128,128]{2,1,0:T(8,128)S(1)} %convolution_add_fusion.5), channel_id=1, source_target_pairs={{0,8},{8,16},{16,24},{24,32},{32,40},{40,48},{48,56},{56,64},{64,7... | collective-permute-start | bytes 786440 | tf_op jit(solution)/shard_map/while/body/eval_jaxpr/ppermute | solution.py:14
  546.6 12.7 %collective-permute-start = (f32[4,128,128]{2,1,0:T(8,128)S(1)}, f32[4,128,128]{2,1,0:T(8,128)S(1)}, u32[]{:S(2)}, u32[]{:S(2)}) collective-permute-start(f32[4,128,128]{2,1,0:T(8,128)S(1)} %convolution_add_fusion.5), channel_id=1, source_target_pairs={{0,8},{8,16},{16,24},{24,32},{32,40},{40,48},{48,56},{56,64},{64,7... | collective-permute-start | bytes 786440 | tf_op jit(solution)/shard_map/while/body/eval_jaxpr/ppermute | solution.py:14
  559.7 12.6 %collective-permute-start = (f32[4,128,128]{2,1,0:T(8,128)S(1)}, f32[4,128,128]{2,1,0:T(8,128)S(1)}, u32[]{:S(2)}, u32[]{:S(2)}) collective-permute-start(f32[4,128,128]{2,1,0:T(8,128)S(1)} %convolution_add_fusion.5), channel_id=1, source_target_pairs={{0,8},{8,16},{16,24},{24,32},{32,40},{40,48},{48,56},{56,64},{64,7... | collective-permute-start | bytes 786440 | tf_op jit(solution)/shard_map/while/body/eval_jaxpr/ppermute | solution.py:14
  572.7 11.7 %collective-permute-start = (f32[4,128,128]{2,1,0:T(8,128)S(1)}, f32[4,128,128]{2,1,0:T(8,128)S(1)}, u32[]{:S(2)}, u32[]{:S(2)}) collective-permute-start(f32[4,128,128]{2,1,0:T(8,128)S(1)} %convolution_add_fusion.5), channel_id=1, source_target_pairs={{0,8},{8,16},{16,24},{24,32},{32,40},{40,48},{48,56},{56,64},{64,7... | collective-permute-start | bytes 786440 | tf_op jit(solution)/shard_map/while/body/eval_jaxpr/ppermute | solution.py:14
  606.3 10.4 %collective-permute-start = (f32[4,128,128]{2,1,0:T(8,128)S(1)}, f32[4,128,128]{2,1,0:T(8,128)S(1)}, u32[]{:S(2)}, u32[]{:S(2)}) collective-permute-start(f32[4,128,128]{2,1,0:T(8,128)S(1)} %convolution_add_fusion.5), channel_id=1, source_target_pairs={{0,8},{8,16},{16,24},{24,32},{32,40},{40,48},{48,56},{56,64},{64,7... | collective-permute-start | bytes 786440 | tf_op jit(solution)/shard_map/while/body/eval_jaxpr/ppermute | solution.py:14
  (7 other events, 207.1 us)
